TPU v7x, 512 devices: a whole 4x4x16 slice. The times are simulated.
512 devices in a mesh: tok: 64 (over z, x), head: 8 (over y, core).
Axes of the slice: x: 4, y: 4, z: 16, core: 2. Of those that a mesh axis runs over, the one named last changes fastest.
Arguments:
- tokens: bfloat16 [32768, 2560], P('tok', 'head'), may hold values from -6 to 6
- query_weight: bfloat16 [2560, 2560], P('tok'), may hold values from -0.125 to 0.125
- keyvalue_weight: bfloat16 [2560, 512], P('tok'), may hold values from -0.125 to 0.125
- output_weight: bfloat16 [2560, 2560], P(None, ('head', 'tok')), may hold values from -0.125 to 0.125
- cache: bfloat16 [2048, 2, 128, 256], P(('tok', 'head')), may hold values from -460 to 460
- page_table: int32 [512, 4], P('tok'), may hold values from 0 to 2047, as said below
- parents: int32 [512, 64], P('tok'), may hold values from 0 to 62, as said below
- cache_len: int32 [512], P('tok'), may hold values from 1 to 448, as said below
- accepted_leaf: int32 [512], P('tok'), may hold values from 0 to 63
Outputs:
- attended: bfloat16 [32768, 2560], P('tok', 'head')
- cache_out: bfloat16 [2048, 2, 128, 256], P(('tok', 'head'))
Inputs may be any that keep to these rules, and one draw needn't show every extreme that they name: `page_table`: for every d, row d names each of the pages d * 4 to d * 4 + 3 exactly once, so request d's pages all lie on device d (devices counted tok-major, head-minor). parents[r, 0] = 0, and parents[r, i] < i for i >= 1. `cache_len`: roughly half of the requests hold at most 128 cached positions, the others more than 320.
All inputs are finite; a program needn't handle non-finite values.
Results may differ from a plain program's by a relative error of at most 0.014.
The roundings to bfloat16 on the way count: a program that leaves them out, or rounds other values in their place, can miss the bound.
Values may be sent and summed in bfloat16 or wider, within the bound.
No kernel may reach another device: no remote copies, remote signals or barrier semaphores. Data moves between devices by JAX's collectives and lax.ppermute only.
A program may use at most 64 MiB of HBM per device.

v0:
```python
import math
import jax
import jax.numpy as jnp
from jax import lax
from jax.sharding import PartitionSpec as P

HQ = 10
HD = 256
DRAFT = 64
PAGE = 128
NPR = 4
WINDOW = 256


def ancestry(parent_row):
    node_ids = jnp.arange(DRAFT, dtype=jnp.int32)
    link = (parent_row[:, None] == node_ids[None, :]).astype(jnp.float32)
    reach = jnp.minimum(link + jnp.eye(DRAFT, dtype=jnp.float32), 1.0)
    for sweep in range((DRAFT - 1).bit_length()):
        reach = jnp.minimum(jnp.dot(reach, reach, precision=lax.Precision.HIGHEST), 1.0)
    depth = (jnp.sum(reach, axis=1) - 1.0).astype(jnp.int32)
    return (reach, depth)


def rotate(values, position):
    half = HD // 4
    freq = jnp.exp(jnp.arange(half, dtype=jnp.float32) * (-2.0 * math.log(10000.0) / (HD // 2)))
    angle = position.astype(jnp.float32)[..., None] * freq
    cosine = jnp.cos(angle)
    sine = jnp.sin(angle)
    first = values[..., :half]
    second = values[..., half : 2 * half]
    return jnp.concatenate(
        [first * cosine - second * sine, second * cosine + first * sine, values[..., 2 * half :]],
        axis=-1,
    )


def attend(queries, cache_keys, cache_values, tree_keys, tree_values, lengths, position, reach):
    window_span = cache_keys.shape[1]
    slot_ids = jnp.arange(window_span, dtype=jnp.int32)
    visible = (slot_ids[None, None, :] < lengths[:, None, None]) & (
        slot_ids[None, None, :] > position[:, :, None] - WINDOW
    )
    cache_scores = jnp.einsum(
        "rnhd,rcd->rhnc", queries, cache_keys, preferred_element_type=jnp.float32
    )
    tree_scores = jnp.einsum(
        "rnhd,rmd->rhnm", queries, tree_keys, preferred_element_type=jnp.float32
    )
    cache_scores = jnp.where(visible[:, None], cache_scores, -1e30)
    tree_scores = jnp.where(reach[:, None] > 0.5, tree_scores, -1e30)
    row_peak = jnp.maximum(jnp.max(cache_scores, axis=-1), jnp.max(tree_scores, axis=-1))[..., None]
    cache_weights = jnp.exp(cache_scores - row_peak)
    tree_weights = jnp.exp(tree_scores - row_peak)
    denominator = jnp.sum(cache_weights, axis=-1, keepdims=True) + jnp.sum(
        tree_weights, axis=-1, keepdims=True
    )
    cache_weights = (cache_weights / denominator).astype(jnp.bfloat16)
    tree_weights = (tree_weights / denominator).astype(jnp.bfloat16)
    result = jnp.einsum(
        "rhnc,rcd->rnhd", cache_weights, cache_values, preferred_element_type=jnp.float32
    )
    result = result + jnp.einsum(
        "rhnm,rmd->rnhd", tree_weights, tree_values, preferred_element_type=jnp.float32
    )
    return result.astype(jnp.bfloat16)


def refresh(logical_pages, length, leaf, reach, depth, new_keys, new_values):
    count = logical_pages.shape[0] * logical_pages.shape[2]
    logical = jnp.transpose(logical_pages, (1, 0, 2, 3)).reshape(2, count, HD)
    slot_ids = jnp.arange(count, dtype=jnp.int32)
    on_path = reach[leaf]
    selector = ((on_path[None, :] > 0.5) & (depth[None, :] == slot_ids[:, None] - length)).astype(
        jnp.float32
    )
    placed_keys = jnp.dot(selector, new_keys.astype(jnp.float32), precision=lax.Precision.HIGHEST)
    placed_values = jnp.dot(
        selector, new_values.astype(jnp.float32), precision=lax.Precision.HIGHEST
    )
    placed = jnp.stack([placed_keys, placed_values]).astype(jnp.bfloat16)
    written = jnp.sum(selector, axis=1) > 0.5
    logical = jnp.where(written[None, :, None], placed, logical)
    return jnp.transpose(
        logical.reshape(2, logical_pages.shape[0], logical_pages.shape[2], HD), (1, 0, 2, 3)
    )


def shards(
    tokens,
    query_weight,
    keyvalue_weight,
    output_weight,
    cache,
    page_table,
    parents,
    cache_len,
    accepted_leaf,
):
    head_count = lax.axis_size("head")
    head_index = lax.axis_index("head")
    tok_index = lax.axis_index("tok")
    requests = parents.shape[0]
    assert requests == head_count
    pages_dev = cache.shape[0]
    part_rows = query_weight.shape[0]
    q_cols = HQ * HD // head_count
    kv_cols = 2 * HD // head_count
    out_cols = output_weight.shape[1]
    wq_piece = lax.dynamic_slice_in_dim(query_weight, head_index * q_cols, q_cols, axis=1)
    wkv_piece = lax.dynamic_slice_in_dim(keyvalue_weight, head_index * kv_cols, kv_cols, axis=1)
    flat = jnp.concatenate([wq_piece.reshape(-1), wkv_piece.reshape(-1), output_weight.reshape(-1)])
    stacked = lax.all_gather(flat, "tok", axis=0, tiled=False)
    tok_count = stacked.shape[0]
    n_q = part_rows * q_cols
    n_kv = part_rows * kv_cols
    wq_cols = stacked[:, :n_q].reshape(tok_count * part_rows, q_cols)
    wkv_cols = stacked[:, n_q : n_q + n_kv].reshape(tok_count * part_rows, kv_cols)
    wo_cols = (
        stacked[:, n_q + n_kv :]
        .reshape(tok_count, HQ * HD, out_cols)
        .transpose(1, 0, 2)
        .reshape(HQ * HD, tok_count * out_cols)
    )
    gathered = lax.all_gather(tokens, "head", axis=1, tiled=True)
    wide = gathered.astype(jnp.float32)
    mean_square = jnp.mean(wide * wide, axis=1, keepdims=True)
    normed = (wide * lax.rsqrt(mean_square + 1e-06)).astype(jnp.bfloat16)
    q_part = jnp.dot(normed, wq_cols, preferred_element_type=jnp.float32)
    kv_part = jnp.dot(normed, wkv_cols, preferred_element_type=jnp.float32)
    both = jnp.concatenate([q_part, kv_part], axis=1)
    mine = lax.all_to_all(both, "head", 0, 1, tiled=True)
    mine = mine.reshape(DRAFT, head_count, q_cols + kv_cols)
    q_pre = mine[:, :, :q_cols].reshape(DRAFT, HQ, HD)
    kv_pre = mine[:, :, q_cols:].reshape(DRAFT, 2 * HD)
    parent_row = lax.dynamic_index_in_dim(parents, head_index, 0, keepdims=False)
    length = lax.dynamic_index_in_dim(cache_len, head_index, 0, keepdims=False)
    leaf = lax.dynamic_index_in_dim(accepted_leaf, head_index, 0, keepdims=False)
    reach, depth = ancestry(parent_row)
    position = length + depth
    queries = (rotate(q_pre, position[:, None]) * HD ** (-0.5)).astype(jnp.bfloat16)
    tree_keys = rotate(kv_pre[:, :HD], position).astype(jnp.bfloat16)
    tree_values = kv_pre[:, HD:].astype(jnp.bfloat16)
    device = tok_index * head_count + head_index
    own_table = (
        lax.dynamic_index_in_dim(page_table, head_index, 0, keepdims=False) - device * pages_dev
    )
    own_pages = jnp.take(cache, own_table, axis=0)
    cache_keys = own_pages[:, 0].reshape(NPR * PAGE, HD)
    cache_values = own_pages[:, 1].reshape(NPR * PAGE, HD)
    result = attend(
        queries[None],
        cache_keys[None],
        cache_values[None],
        tree_keys[None],
        tree_values[None],
        length[None],
        position[None],
        reach[None],
    )
    mixed = lax.all_gather(result.reshape(DRAFT, HQ * HD), "head", axis=0, tiled=True)
    summed = jnp.zeros((mixed.shape[0], wo_cols.shape[1]), jnp.float32)
    for group in range(head_count):
        head_ids = [k for k in range(group, HQ, head_count)]
        if not head_ids:
            continue
        columns = jnp.concatenate([mixed[:, k * HD : (k + 1) * HD] for k in head_ids], axis=1)
        rows = jnp.concatenate([wo_cols[k * HD : (k + 1) * HD] for k in head_ids], axis=0)
        partial_value = jnp.dot(columns, rows, preferred_element_type=jnp.float32)
        summed = summed + partial_value.astype(jnp.bfloat16).astype(jnp.float32)
    attended = summed.astype(jnp.bfloat16)
    new_pages = refresh(own_pages, length, leaf, reach, depth, tree_keys, tree_values)
    matches = (own_table[:, None] == jnp.arange(pages_dev, dtype=jnp.int32)[None, :]).astype(
        jnp.int32
    )
    inverse = jnp.sum(matches * jnp.arange(pages_dev, dtype=jnp.int32)[:, None], axis=0)
    cache_out = jnp.take(new_pages, inverse, axis=0)
    return (attended, cache_out)


def solution(mesh):
    in_specs = (
        P("tok", "head"),
        P("tok", None),
        P("tok", None),
        P(None, ("head", "tok")),
        P(("tok", "head"), None, None, None),
        P("tok", None),
        P("tok", None),
        P("tok"),
        P("tok"),
    )
    out_specs = (P("tok", "head"), P(("tok", "head"), None, None, None))
    return jax.shard_map(shards, mesh=mesh, in_specs=in_specs, out_specs=out_specs, check_vma=False)
```

profile of v0, /device:TPU:1, one launch (start us, length us, event | category | flops | bytes accessed | tf_op | source)
XLA Modules:
  0.0 285.6 jit_solution(11939136876773440064)
XLA Ops:
  7.2 0.7 all-gather.6.cloned.1.call-update
  8.0 0.9 constant_dynamic-slice_fusion.2
  9.0 0.8 constant_dynamic-slice_fusion.1
  9.8 1.2 copy.62
  11.0 1.0 reshape.334
  12.0 0.7 reshape.362
  12.7 1.3 dynamic_slice.29
  15.4 1.2 dynamic_slice.25
  16.7 0.7 fusion.70
  19.5 0.7 iota_subtract_fusion
  20.4 29.1 %all-gather.6.cloned.1.call-done = bf16[512,2560]{0,1:T(8,128)(2,1)} async-done(((bf16[512,320]{0,1:T(8,128)(2,1)}), bf16[512,2560]{0,1:T(8,128)(2,1)}) %all-gather.6.cloned.1.call-update) | async-done | bytes 2621456 | tf_op jit(solution)/shard_map/all_gather | solution.py:126
  49.5 2.4 fusion
  51.9 146.4 %all-gather.10.cloned.1.call-done = bf16[64,1,28160]{2,1,0:T(2,128)(2,1)} async-done(((bf16[1,1,28160]{2,1,0:T(2,128)(2,1)}), bf16[64,1,28160]{2,1,0:T(2,128)(2,1)}) %all-gather.10.cloned.1.call-update) | async-done | bytes 3604496 | tf_op jit(solution)/shard_map/all_gather | solution.py:114
  198.3 3.5 %copy.97 = bf16[64,1,28160]{2,0,1:T(8,128)(2,1)S(1)} copy(bf16[64,1,28160]{2,1,0:T(2,128)(2,1)} %all-gather.10.cloned.1.call-done) | data formatting | bytes 7208960
  201.7 1.4 fusion.79
  203.1 2.5 reshape.335
  205.6 0.4 reshape.336
  206.0 3.6 %fusion.4 = f32[512,320]{0,1:T(8,128)S(1)} fusion(bf16[2560,320]{1,0:T(8,128)(2,1)} %reshape.335, bf16[512,2560]{0,1:T(8,128)(2,1)} %all-gather.6.cloned.1.call-done, f32[512]{0:T(512)S(1)} %add_rsqrt_fusion), kind=kOutput, calls=%fused_computation.8 | convolution fusion | flops 842792960 | bytes 4917248 | tf_op jit(solution)/shard_map/dot_general | solution.py:130
  209.7 0.7 fusion.2
  210.5 1.2 copy.63
  211.6 12.7 %all-to-all-start = ((f32[8,64,384]{2,1,0:T(8,128)}), f32[8,64,384]{2,1,0:T(8,128)S(1)}, u32[]{:S(2)}, u32[]{:S(2)}) async-start(f32[8,64,384]{2,1,0:T(8,128)} %bitcast.6), calls=%async_computation | async-start | bytes 1572864 | tf_op jit(solution)/shard_map/all_to_all | solution.py:133
  224.3 0.6 iota_compare_fusion.6
  225.1 0.6 gather_fusion
  225.7 0.7 add_add_fusion
  226.4 10.0 %all-to-all-done = f32[8,64,384]{2,1,0:T(8,128)S(1)} async-done(((f32[8,64,384]{2,1,0:T(8,128)}), f32[8,64,384]{2,1,0:T(8,128)S(1)}, u32[]{:S(2)}, u32[]{:S(2)}) %all-to-all-start) | async-done | bytes 786464 | tf_op jit(solution)/shard_map/all_to_all | solution.py:133
  236.9 0.3 convolution_convert_fusion.8
  237.3 0.5 copy.64
  237.7 0.4 reshape.337
  238.6 0.3 convolution_convert_fusion.9
  239.0 1.0 fusion.36
  240.3 0.4 fusion.84
  240.7 0.5 fusion.83
  241.3 0.4 fusion.26
  241.7 0.3 fusion.50
  242.0 0.4 fusion.85
  242.5 0.7 copy.90
  243.5 2.9 %copy.72 = bf16[64,12800]{0,1:T(8,128)(2,1)} copy(bf16[64,12800]{1,0:T(8,128)(2,1)S(1)} %copy-done.1) | data formatting | bytes 3276800 | tf_op jit(solution)/shard_map/slice | solution.py:121
  246.4 7.1 %reshape.342 = bf16[64,2560,5]{0,2,1:T(8,128)(2,1)} reshape(bf16[64,12800]{0,1:T(8,128)(2,1)} %copy.72) | data formatting | bytes 3276800 | tf_op jit(solution)/shard_map/reshape | solution.py:122
  253.5 4.9 %fusion.78 = (bf16[256,64,5]{1,2,0:T(8,128)(2,1)S(1)}, bf16[256,64,5]{1,2,0:T(8,128)(2,1)S(1)}, bf16[256,64,5]{1,2,0:T(8,128)(2,1)S(1)}, bf16[256,64,5]{1,2,0:T(...) fusion(bf16[2560,64,5]{1,2,0:T(8,128)(2,1)} %bitcast.112), kind=kLoop, calls=%fused_computation.143 | loop fusion | bytes 3276800 | tf_op jit(solution)/shard_map/slice | solution.py:169
  258.4 1.5 copy.73
  259.9 0.7 slice.155
  260.7 1.5 copy.74
  262.1 0.7 slice.157
  262.9 1.5 copy.75
  264.4 0.7 slice.161
  265.1 1.5 copy.76
  266.6 0.7 slice.163
  267.4 1.5 copy.77
  268.9 0.7 slice.166
  269.6 0.4 copy.78
  270.0 0.7 slice.169
  270.8 0.4 copy.79
  271.3 0.4 copy.80
  271.8 0.4 copy.81
  272.4 0.4 copy.82
  272.9 0.6 gather_fusion.1
  273.5 0.9 broadcast_select_fusion
  274.4 1.4 fusion.80
  275.9 0.4 fusion.23
  276.3 0.4 fusion.22
  277.2 0.3 fusion.16
  277.5 0.3 fusion.14
  277.8 0.3 fusion.12
  278.1 1.0 fusion.10
  (77 shorter events, 4.6 us)
Async XLA Ops:
  7.2 217.9 %copy-start = (bf16[4,2,128,256]{3,2,1,0:T(8,128)(2,1)S(1)}, bf16[4,2,128,256]{3,2,1,0:T(8,128)(2,1)}, u32[]{:S(2)}) copy-start(bf16[4,2,128,256]{3,2,1,0:T(8,128)(2,1)} %param.15) | copy-start | bytes 1572868
  7.2 12.1 %copy-start.11 = (s32[8,4]{0,1:T(4,128)S(1)}, s32[8,4]{0,1:T(4,128)}, u32[]{:S(2)}) copy-start(s32[8,4]{0,1:T(4,128)} %param.16) | copy-start | bytes 388
  7.2 42.3 %all-gather.6.cloned.1.call-start = ((), (), s32[]{:S(2)}) async-start(), calls=%async_computation.1 | async-start | bytes 2949120 | tf_op jit(solution)/shard_map/all_gather | solution.py:126
  7.9 190.3 %all-gather.10.cloned.1.call-start = ((), (), s32[]{:S(2)}) async-start(), calls=%async_computation.3 | async-start | bytes 7321600 | tf_op jit(solution)/shard_map/all_gather | solution.py:114
  206.0 3.7 %copy-start.2 = (bf16[512,2560]{0,1:T(8,128)(2,1)S(1)}, bf16[512,2560]{0,1:T(8,128)(2,1)}, u32[]{:S(2)}) copy-start(bf16[512,2560]{0,1:T(8,128)(2,1)} %all-gather.6.cloned.1.call-done) | copy-start | bytes 7864324
  211.6 24.9 %all-to-all-start = ((f32[8,64,384]{2,1,0:T(8,128)}), f32[8,64,384]{2,1,0:T(8,128)S(1)}, u32[]{:S(2)}, u32[]{:S(2)}) async-start(f32[8,64,384]{2,1,0:T(8,128)} %bitcast.6), calls=%async_computation | async-start | bytes 1572864 | tf_op jit(solution)/shard_map/all_to_all | solution.py:133
  224.3 50.1 %all-gather.8.cloned.1.call-start = ((), (), s32[]{:S(2)}) async-start(), calls=%async_computation.2 | async-start | bytes 2949120 | tf_op jit(solution)/shard_map/all_gather | solution.py:162
  242.0 1.5 copy-start.1
  270.0 2.9 %copy-start.4 = (bf16[4,2,128,256]{3,2,1,0:T(8,128)(2,1)S(1)}, bf16[4,2,128,256]{3,2,1,0:T(8,128)(2,1)}, u32[]{:S(2)}) copy-start(bf16[4,2,128,256]{3,2,1,0:T(8,128)(2,1)} %get-tuple-element.3) | copy-start | bytes 1572868
  272.3 3.5 %copy-start.9 = (bf16[256,320]{0,1:T(8,128)(2,1)S(1)}, bf16[256,320]{0,1:T(8,128)(2,1)}, u32[]{:S(2)}) copy-start(bf16[256,320]{0,1:T(8,128)(2,1)} %slice.155) | copy-start | bytes 491524
  272.4 3.5 %copy-start.10 = (bf16[256,320]{0,1:T(8,128)(2,1)S(1)}, bf16[256,320]{0,1:T(8,128)(2,1)}, u32[]{:S(2)}) copy-start(bf16[256,320]{0,1:T(8,128)(2,1)} %slice.157) | copy-start | bytes 491524
  273.5 2.8 copy-start.5
  273.5 2.8 copy-start.6
  274.4 2.2 copy-start.7
  274.4 2.2 copy-start.3
  275.9 1.1 copy-start.8
Sparse Core Ops, SparseCore 0:
  10.1 39.3 all-gather.5
  53.1 145.1 all-gather.9
  243.4 27.9 all-gather.7
where the time goes:
time: 287 us; the launch traced here: 286 us
  waiting for transfers between devices  186 us (65%)
  local copies, waits for them, and re-layouts  51.5 us (18%)
  between operations  16.5 us (6%)
  starting transfers between devices  12.8 us (4%)
  matrix products  10.8 us (4%)
  other arithmetic  7.81 us (3%)
    all_gather x1, waiting for transfers between devices, shards(): stacked = lax.all_gather(flat, 'tok', axis=0, tiled=False)  146 us
    all_gather x1, waiting for transfers between devices, shards(): gathered = lax.all_gather(tokens, 'head', axis=1, tiled=True)  29.1 us
    slice x21, local copies, waits for them, and re-layouts, shards(): wo_cols[k * HD:(k + 1) * HD]  19.2 us
    all_to_all x1, starting transfers between devices, shards(): mine = lax.all_to_all(both, 'head', 0, 1, tiled=True)  12.7 us
    all_to_all x1, waiting for transfers between devices, shards(): mine = lax.all_to_all(both, 'head', 0, 1, tiled=True)  10 us
    reshape x1, local copies, waits for them, and re-layouts, shards(): wo_cols = stacked[:, n_q + n_kv:].reshape(tok_count, HQ * HD, out_cols).t...  7.08 us
    unnamed x29, local copies, waits for them, and re-layouts  6.45 us
  transfers between devices with their start and end apart: 4, of which 3 were waited for; matrix products, arithmetic and copies ran while one was open for 16% of the time, Pallas kernels for 0%

commit v1 on v0

--- a/solution.py
+++ b/solution.py
@@ -98,6 +98,12 @@
     cache_len,
     accepted_leaf,
 ):
+
+    def fix_paths_by_axis(mat):
+        front = jnp.concatenate(lax.axis_size("head") * [mat], axis=1)
+        then = lax.all_to_all(front, axis_name="head", split_axis=1, concat_axis=1, tiled=True)
+        return then
+
     head_count = lax.axis_size("head")
     head_index = lax.axis_index("head")
     tok_index = lax.axis_index("tok")
@@ -123,7 +129,7 @@
         .transpose(1, 0, 2)
         .reshape(HQ * HD, tok_count * out_cols)
     )
-    gathered = lax.all_gather(tokens, "head", axis=1, tiled=True)
+    gathered = fix_paths_by_axis(tokens)
     wide = gathered.astype(jnp.float32)
     mean_square = jnp.mean(wide * wide, axis=1, keepdims=True)
     normed = (wide * lax.rsqrt(mean_square + 1e-06)).astype(jnp.bfloat16)

time: 287 us -> 251 us (0.87)
  waiting for transfers between devices: 186 us -> 138 us
  starting transfers between devices: 12.8 us -> 23.2 us
    all_gather x1, waiting for transfers between devices: 146 us -> 103 us  [shards(): stacked = lax.all_gather(flat, 'tok', axis=0, tiled=False)]
    all_gather x1 -> x0, waiting for transfers between devices: 29.1 us -> none  [shards(): gathered = lax.all_gather(tokens, 'head', axis=1, tiled=True)]
    all_to_all x0 -> x1, waiting for transfers between devices: none -> 25 us  [fix_paths_by_axis(): lax.all_to_all(front, axis_name='head', split_axis=1, concat_axis=1, tile...]
    all_to_all x0 -> x1, starting transfers between devices: none -> 10.5 us  [fix_paths_by_axis(): lax.all_to_all(front, axis_name='head', split_axis=1, concat_axis=1, tile...]
    unnamed x29 -> x44, local copies, waits for them, and re-layouts: 6.45 us -> 9.23 us
  transfers between devices with their start and end apart: 4 -> 4, of which waited for: 3 -> 3; matrix products, arithmetic and copies ran while one was open for 16% -> 15% of each run, Pallas kernels for 0% -> 0%
where the time goes in v1:
time: 251 us; the launch traced here: 250 us
  waiting for transfers between devices  138 us (55%)
  local copies, waits for them, and re-layouts  53.8 us (21%)
  starting transfers between devices  23.2 us (9%)
  between operations  16.7 us (7%)
  matrix products  9.73 us (4%)
  other arithmetic  8.16 us (3%)
    all_gather x1, waiting for transfers between devices, shards(): stacked = lax.all_gather(flat, 'tok', axis=0, tiled=False)  103 us
    all_to_all x1, waiting for transfers between devices, fix_paths_by_axis(): lax.all_to_all(front, axis_name='head', split_axis=1, concat_axis=1, tile...  25 us
    slice x21, local copies, waits for them, and re-layouts, shards(): wo_cols[k * HD:(k + 1) * HD]  16.9 us
    all_to_all x1, starting transfers between devices, shards(): mine = lax.all_to_all(both, 'head', 0, 1, tiled=True)  12.7 us
    all_to_all x1, waiting for transfers between devices, shards(): mine = lax.all_to_all(both, 'head', 0, 1, tiled=True)  10.7 us
    all_to_all x1, starting transfers between devices, fix_paths_by_axis(): lax.all_to_all(front, axis_name='head', split_axis=1, concat_axis=1, tile...  10.5 us
    unnamed x44, local copies, waits for them, and re-layouts  9.23 us
    reshape x1, local copies, waits for them, and re-layouts, shards(): wo_cols = stacked[:, n_q + n_kv:].reshape(tok_count, HQ * HD, out_cols).t...  7.08 us
  transfers between devices with their start and end apart: 4, of which 3 were waited for; matrix products, arithmetic and copies ran while one was open for 15% of the time, Pallas kernels for 0%

profile of v1, /device:TPU:1, one launch (start us, length us, event | category | flops | bytes accessed | tf_op | source)
XLA Modules:
  0.0 249.8 jit_solution(2795153089188521090)
XLA Ops:
  7.2 0.9 constant_dynamic-slice_fusion.1
  8.2 0.9 constant_dynamic-slice_fusion.2
  9.2 1.2 copy.62
  10.3 1.0 reshape.348
  11.3 0.7 reshape.376
  12.1 1.0 constant_dynamic-update-slice_fusion.7
  13.3 1.6 copy-done.5
  14.9 10.5 %all-to-all-start = ((bf16[512,8,320]{0,2,1:T(8,128)(2,1)}), bf16[512,8,320]{0,2,1:T(8,128)(2,1)S(1)}, u32[]{:S(2)}, u32[]{:S(2)}) async-start(bf16[512,8,320]{0,2,1:T(8,128)(2,1)} %bitcast.123), calls=%async_computation | async-start | bytes 5242880 | tf_op jit(solution)/shard_map/all_to_all | solution.py:104
  25.4 0.7 fusion.66
  26.5 0.7 dynamic_slice.29
  28.4 0.6 dynamic_slice.25
  30.6 0.7 iota_compare_fusion.6
  31.3 0.7 iota_subtract_fusion
  32.2 25.0 %all-to-all-done = bf16[512,8,320]{0,2,1:T(8,128)(2,1)S(1)} async-done(((bf16[512,8,320]{0,2,1:T(8,128)(2,1)}), bf16[512,8,320]{0,2,1:T(8,128)(2,1)S(1)}, u32[]{:S(2)}, u32[]{:S(2)}) %all-to-all-start) | async-done | bytes 2621472 | tf_op jit(solution)/shard_map/all_to_all | solution.py:104
  57.2 0.6 fusion
  57.8 2.1 fusion.1
  59.9 102.5 %all-gather.7.cloned.1.call-done = bf16[64,1,28160]{2,1,0:T(2,128)(2,1)} async-done(((bf16[1,1,28160]{2,1,0:T(2,128)(2,1)}), bf16[64,1,28160]{2,1,0:T(2,128)(2,1)}) %all-gather.7.cloned.1.call-update) | async-done | bytes 3604496 | tf_op jit(solution)/shard_map/all_gather | solution.py:120
  162.4 3.5 %copy.97 = bf16[64,1,28160]{2,0,1:T(8,128)(2,1)S(1)} copy(bf16[64,1,28160]{2,1,0:T(2,128)(2,1)} %all-gather.7.cloned.1.call-done) | data formatting | bytes 7208960
  165.9 1.9 fusion.75
  167.9 1.2 reshape.350
  169.1 4.1 %reshape.349 = bf16[2560,320]{1,0:T(8,128)(2,1)} reshape(bf16[64,12800]{1,0:T(8,128)(2,1)} %get-tuple-element.16) | data formatting | bytes 3276800 | tf_op jit(solution)/shard_map/reshape | solution.py:124
  173.2 2.7 %fusion.84 = f32[512,320]{0,1:T(8,128)S(1)} fusion(bf16[512,2560]{0,1:T(8,128)(2,1)S(1)} %bitcast.119, bf16[2560,320]{1,0:T(8,128)(2,1)} %reshape.349), kind=kOutput, calls=%fused_computation.157 | convolution fusion | flops 838860800 | bytes 4915200 | tf_op jit(solution)/shard_map/dot_general | solution.py:136
  176.0 0.6 fusion.85
  176.6 1.2 copy.63
  177.7 12.7 %all-to-all-start.1 = ((f32[8,64,384]{2,1,0:T(8,128)}), f32[8,64,384]{2,1,0:T(8,128)S(1)}, u32[]{:S(2)}, u32[]{:S(2)}) async-start(f32[8,64,384]{2,1,0:T(8,128)} %bitcast.8), calls=%async_computation.1 | async-start | bytes 1572864 | tf_op jit(solution)/shard_map/all_to_all | solution.py:139
  190.6 0.6 gather_fusion
  191.2 0.7 add_add_fusion
  191.9 10.7 %all-to-all-done.1 = f32[8,64,384]{2,1,0:T(8,128)S(1)} async-done(((f32[8,64,384]{2,1,0:T(8,128)}), f32[8,64,384]{2,1,0:T(8,128)S(1)}, u32[]{:S(2)}, u32[]{:S(2)}) %all-to-all-start.1) | async-done | bytes 786464 | tf_op jit(solution)/shard_map/all_to_all | solution.py:139
  203.0 0.3 convolution_convert_fusion.8
  203.4 0.5 copy.64
  203.9 0.4 reshape.351
  204.8 0.3 convolution_convert_fusion.9
  205.1 1.0 fusion.32
  206.4 0.4 fusion.80
  206.8 0.5 fusion.79
  207.4 0.4 fusion.22
  207.9 0.3 fusion.46
  208.2 0.4 fusion.81
  208.6 0.7 copy.90
  209.6 2.9 %copy.72 = bf16[64,12800]{0,1:T(8,128)(2,1)} copy(bf16[64,12800]{1,0:T(8,128)(2,1)S(1)} %copy-done.4) | data formatting | bytes 3276800 | tf_op jit(solution)/shard_map/slice | solution.py:127
  212.6 7.1 %reshape.356 = bf16[64,2560,5]{0,2,1:T(8,128)(2,1)} reshape(bf16[64,12800]{0,1:T(8,128)(2,1)} %copy.72) | data formatting | bytes 3276800 | tf_op jit(solution)/shard_map/reshape | solution.py:128
  219.6 5.0 %fusion.74 = (bf16[256,64,5]{1,2,0:T(8,128)(2,1)}, bf16[256,64,5]{1,2,0:T(8,128)(2,1)}, bf16[256,64,5]{1,2,0:T(8,128)(2,1)}, bf16[256,64,5]{1,2,0:T(8,128)(2,1)}...) fusion(bf16[2560,64,5]{1,2,0:T(8,128)(2,1)} %bitcast.116), kind=kLoop, calls=%fused_computation.149 | loop fusion | bytes 3276800 | tf_op jit(solution)/shard_map/slice | solution.py:175
  224.6 1.5 copy.82
  226.1 0.7 slice.181
  226.8 1.5 copy.81
  228.3 0.7 slice.178
  229.0 1.5 copy.80
  230.6 0.7 slice.175
  231.3 1.5 copy.79
  232.8 0.8 slice.172
  233.5 0.4 copy.78
  234.1 0.4 copy.77
  234.6 0.4 copy.76
  235.1 0.4 copy.75
  235.7 0.4 copy.74
  236.2 0.4 copy.73
  236.7 0.6 gather_fusion.1
  237.3 0.9 broadcast_select_fusion
  238.2 1.4 fusion.76
  239.7 0.4 fusion.19
  240.0 0.4 fusion.18
  240.7 0.3 fusion.14
  241.0 0.3 fusion.12
  242.0 1.0 fusion.6
  (93 shorter events, 5.2 us)
Async XLA Ops:
  7.2 183.4 %copy-start = (bf16[4,2,128,256]{3,2,1,0:T(8,128)(2,1)S(1)}, bf16[4,2,128,256]{3,2,1,0:T(8,128)(2,1)}, u32[]{:S(2)}) copy-start(bf16[4,2,128,256]{3,2,1,0:T(8,128)(2,1)} %param.15) | copy-start | bytes 1572868
  7.2 5.9 %copy-start.2 = (bf16[512,320]{0,1:T(8,128)(2,1)S(1)}, bf16[512,320]{0,1:T(8,128)(2,1)}, u32[]{:S(2)}) copy-start(bf16[512,320]{0,1:T(8,128)(2,1)} %param.11) | copy-start | bytes 983044
  7.2 155.3 %all-gather.7.cloned.1.call-start = ((), (), s32[]{:S(2)}) async-start(), calls=%async_computation.3 | async-start | bytes 7321600 | tf_op jit(solution)/shard_map/all_gather | solution.py:120
  13.3 1.6 copy-start.5
  14.8 11.6 %copy-start.14 = (s32[8]{0:T(128)S(1)}, s32[8]{0:T(128)}, u32[]{:S(2)}) copy-start(s32[8]{0:T(128)} %param.19) | copy-start | bytes 100
  14.9 13.6 %copy-start.15 = (s32[8]{0:T(128)S(1)}, s32[8]{0:T(128)}, u32[]{:S(2)}) copy-start(s32[8]{0:T(128)} %param.18) | copy-start | bytes 100
  14.9 15.6 %copy-start.13 = (s32[8,4]{0,1:T(4,128)S(1)}, s32[8,4]{0,1:T(4,128)}, u32[]{:S(2)}) copy-start(s32[8,4]{0,1:T(4,128)} %param.16) | copy-start | bytes 388
  14.9 42.3 %all-to-all-start = ((bf16[512,8,320]{0,2,1:T(8,128)(2,1)}), bf16[512,8,320]{0,2,1:T(8,128)(2,1)S(1)}, u32[]{:S(2)}, u32[]{:S(2)}) async-start(bf16[512,8,320]{0,2,1:T(8,128)(2,1)} %bitcast.123), calls=%async_computation | async-start | bytes 5242880 | tf_op jit(solution)/shard_map/all_to_all | solution.py:104
  167.9 5.4 %copy-start.3 = (bf16[512,8,320]{0,2,1:T(8,128)(2,1)S(1)}, bf16[512,8,320]{0,2,1:T(8,128)(2,1)}, u32[]{:S(2)}) copy-start(bf16[512,8,320]{0,2,1:T(8,128)(2,1)} %fusion.1) | copy-start | bytes 7864324
  173.2 2.7 %copy-start.7 = (bf16[2560,64]{1,0:T(8,128)(2,1)S(1)}, bf16[2560,64]{1,0:T(8,128)(2,1)}, u32[]{:S(2)}) copy-start(bf16[2560,64]{1,0:T(8,128)(2,1)} %reshape.350) | copy-start | bytes 983044
  177.7 24.9 %all-to-all-start.1 = ((f32[8,64,384]{2,1,0:T(8,128)}), f32[8,64,384]{2,1,0:T(8,128)S(1)}, u32[]{:S(2)}, u32[]{:S(2)}) async-start(f32[8,64,384]{2,1,0:T(8,128)} %bitcast.8), calls=%async_computation.1 | async-start | bytes 1572864 | tf_op jit(solution)/shard_map/all_to_all | solution.py:139
  190.4 47.8 %all-gather.5.cloned.1.call-start = ((), (), s32[]{:S(2)}) async-start(), calls=%async_computation.2 | async-start | bytes 2949120 | tf_op jit(solution)/shard_map/all_gather | solution.py:168
  208.2 1.5 copy-start.4
  234.5 2.2 copy-start.8
  238.2 2.2 copy-start.6
  240.0 1.0 copy-start.12
  240.4 0.9 copy-start.11
  240.7 0.9 copy-start.10
  241.0 1.0 copy-start.9
  241.0 2.0 copy-start.1
Sparse Core Ops, SparseCore 0:
  12.2 150.2 all-gather.6
  209.5 27.9 all-gather.4
